TPU v7x, 512 devices: a whole 4x4x16 slice. The times are simulated.
512 devices in a mesh: row: 32 (over x_lo, z), col: 16 (over x_hi, y, core).
Axes of the slice: x: 4 (x_hi: 2, x_lo: 2; x = x_hi * 2 + x_lo), y: 4, z: 16, core: 2. Of those that a mesh axis runs over, the one named last changes fastest.
Arguments:
- anc_inv: float32 [12288, 12288], P('row', 'col'), may hold values from -0.0546875 to 0.0546875
- factors_first: float32 [3, 256, 12288], P(None, 'row', 'col'), may hold values from -6 to 6
- factors_second: float32 [2, 256, 12288], P(None, 'row', 'col'), may hold values from -6 to 6
- lists_first: int32 [3, 36], replicated, may hold values from 0 to 47, as said below
- lists_second: int32 [2, 36], replicated, may hold values from 0 to 47, as said below
- parents: int32 [2], replicated, may hold values from 0 to 2, as said below
- parent_link: float32 [2, 256, 256], replicated, may hold values from -0.375 to 0.375
Outputs:
- first_cols: float32 [3, 256, 12288], P(None, 'col', 'row')
- second_cols: float32 [2, 256, 12288], P(None, 'col', 'row')
Inputs may be any that keep to these rules, and one draw needn't show every extreme that they name: `lists_first`: each row holds 36 different tile indices. `lists_second`: each row holds 36 different tile indices. `parents`: the 2 entries are different first-generation indices.
All inputs are finite; a program needn't handle non-finite values.
Results may differ from a plain program's by a relative error of at most 0.000084.
Values sent between devices are 32-bit elements; how exact they have to be, the bound alone decides.
No kernel may reach another device: no remote copies, remote signals or barrier semaphores. Data moves between devices by JAX's collectives and lax.ppermute only.
A program may use at most 64 MiB of HBM per device.

v0:
```python
import jax
import jax.numpy as jnp
from jax import lax
from jax.sharding import PartitionSpec as P

highest = lax.Precision.HIGHEST


def tile_flags(block_lists, anchor, extent, tile_height):
    tile_ids = (anchor + jnp.arange(extent, dtype=jnp.int32)) // tile_height
    matches = block_lists[:, :, None] == tile_ids[None, None, :]
    return jnp.any(matches, axis=1).astype(jnp.float32)


def local(anc_inv, factors_first, factors_second, lists_first, lists_second, parents, parent_link):
    local_rows, local_cols = anc_inv.shape
    n_first = factors_first.shape[0]
    n_second = factors_second.shape[0]
    members = n_first + n_second
    share_rows = factors_first.shape[1]
    panel_width = parent_link.shape[1]
    row_anchor = lax.axis_index("row") * local_rows
    col_anchor = lax.axis_index("col") * local_cols
    out_first = tile_flags(lists_first, row_anchor, local_rows, panel_width)
    out_second = tile_flags(lists_second, row_anchor, local_rows, panel_width)
    panels = jnp.concatenate(
        [
            factors_first
            * tile_flags(lists_first, col_anchor, local_cols, panel_width)[:, None, :],
            factors_second
            * tile_flags(lists_second, col_anchor, local_cols, panel_width)[:, None, :],
        ],
        axis=0,
    )
    stacked = jnp.transpose(panels, (1, 0, 2)).reshape(share_rows, members * local_cols)
    gathered = lax.all_gather(stacked, "row", axis=0, tiled=True)
    gathered = gathered.reshape(panel_width, members, local_cols)
    partial_value = jnp.einsum(
        "kmj,ij->mki", gathered, anc_inv, precision=highest, preferred_element_type=jnp.float32
    )
    first_partial = partial_value[:n_first]
    second_partial = partial_value[n_first:]
    chosen = jnp.take(first_partial, parents, axis=0)
    chosen_mask = jnp.take(out_first, parents, axis=0)
    coupling = jnp.einsum("cqk,cqi->cki", parent_link, chosen, precision=highest)
    second_partial = second_partial - chosen_mask[:, None, :] * coupling
    combined = jnp.concatenate([first_partial, second_partial], axis=0)
    reduced = lax.psum_scatter(combined, "col", scatter_dimension=1, tiled=True)
    first_cols = -out_first[:, None, :] * reduced[:n_first]
    second_cols = -out_second[:, None, :] * reduced[n_first:]
    return (first_cols, second_cols)


def solution(mesh):
    in_specs = (P("row", "col"), P(None, "row", "col"), P(None, "row", "col"), P(), P(), P(), P())
    out_specs = (P(None, "col", "row"), P(None, "col", "row"))
    return jax.shard_map(local, mesh=mesh, in_specs=in_specs, out_specs=out_specs, check_vma=False)
```

profile of v0, /device:TPU:8, one launch (start us, length us, event | category | flops | bytes accessed | tf_op | source)
XLA Modules:
  0.0 276.0 jit_solution(1879956316999210277)
XLA Ops:
  7.2 0.0 copy-start
  7.2 0.0 all-gather.2.cloned.1.call-start
  7.2 0.9 compare_reduce_fusion
  8.2 0.8 compare_reduce_fusion.1
  9.0 0.9 broadcast_multiply_fusion
  9.9 0.8 broadcast_multiply_fusion.1
  10.7 0.6 pad_maximum_fusion.1
  11.3 0.0 all-gather.2.cloned.1.call-update
  11.3 0.0 reduce-scatter.2.cloned.1.call-start
  11.4 0.8 compare_reduce_fusion.2
  12.2 0.7 compare_select_fusion
  12.9 0.6 gather_fusion
  13.4 0.7 compare_and_fusion
  14.1 0.1 broadcast_select_fusion
  14.2 139.4 %all-gather.2.cloned.1.call-done = f32[256,3840]{1,0:T(8,128)} async-done(((f32[8,3840]{1,0:T(8,128)}), f32[256,3840]{1,0:T(8,128)}) %all-gather.2.cloned.1.call-update) | async-done | bytes 3932176 | tf_op jit(solution)/shard_map/all_gather | solution.py:36
  153.6 5.4 %copy.19 = f32[256,3840]{0,1:T(8,128)} copy(f32[256,3840]{1,0:T(8,128)} %all-gather.2.cloned.1.call-done) | data formatting | bytes 7864320 | tf_op jit(solution)/shard_map/all_gather | solution.py:36
  159.1 0.0 copy-done
  159.1 14.7 %convolution_bitcast_fusion = f32[5,256,384]{2,1,0:T(8,128)S(1)} fusion(f32[256,5,768]{0,2,1:T(8,128)} %bitcast.15, f32[384,768]{1,0:T(8,128)S(1)} %copy-done), kind=kOutput, calls=%fused_computation.3 | convolution fusion | flops 4529848320 | bytes 7077888 | tf_op jit(solution)/shard_map/kmj,ij->mki/dot_general | solution.py:38
  173.8 0.0 copy-start.1
  173.8 1.3 copy-done.1
  175.1 0.1 slice.20
  175.1 0.6 gather_fusion.1
  175.8 2.5 fusion.1
  178.3 1.4 pad_maximum_fusion
  179.7 0.0 copy-start.2
  179.7 0.0 reduce-scatter.2.cloned.1.call-update
  179.7 0.7 copy-done.2
  180.4 0.1 compare_reduce_fusion.3
  180.5 85.7 %reduce-scatter.2.cloned.1.call-done = f32[5,16,384]{2,1,0:T(8,128)} async-done(((f32[5,256,384]{2,1,0:T(8,128)}), f32[5,16,384]{2,1,0:T(8,128)}) %reduce-scatter.2.cloned.1.call-update) | async-done | bytes 122896 | tf_op jit(solution)/shard_map/reduce_scatter | solution.py:48
  266.2 1.5 slice_multiply_fusion
  267.7 1.4 slice_multiply_fusion.1
  (8 shorter events, 0.1 us)
Async XLA Ops:
  7.2 151.9 %copy-start = (f32[384,768]{1,0:T(8,128)S(1)}, f32[384,768]{1,0:T(8,128)}, u32[]{:S(2)}) copy-start(f32[384,768]{1,0:T(8,128)} %param.7) | copy-start | bytes 3538948
  7.2 146.4 %all-gather.2.cloned.1.call-start = ((), (), s32[]{:S(2)}) async-start(), calls=%async_computation.1 | async-start | bytes 4055040 | tf_op jit(solution)/shard_map/all_gather | solution.py:36
  11.3 254.9 %reduce-scatter.2.cloned.1.call-start = ((), (), s32[]{:S(2)}) async-start(), calls=%async_computation.2 | async-start | bytes 2088960 | tf_op jit(solution)/shard_map/reduce_scatter | solution.py:48
  173.8 1.3 copy-start.1
  179.7 0.7 copy-start.2
Sparse Core Ops, SparseCore 0:
  11.5 142.1 all-gather.1
  179.8 86.3 reduce-scatter.1
where the time goes:
time: 277 us; the launch traced here: 276 us
  waiting for transfers between devices  225 us (81%)
  matrix products  17.2 us (6%)
  between operations  14.2 us (5%)
  other arithmetic  10.7 us (4%)
  local copies, waits for them, and re-layouts  8.62 us (3%)
    all_gather x1, waiting for transfers between devices, local(): gathered = lax.all_gather(stacked, 'row', axis=0, tiled=True)  139 us
    reduce_scatter x1, waiting for transfers between devices, local(): reduced = lax.psum_scatter(combined, 'col', scatter_dimension=1, tiled=True)  85.7 us
    dot_general x1, matrix products, local(): jnp.einsum('kmj,ij->mki', gathered, anc_inv, precision=highest, preferred...  14.7 us
  transfers between devices with their start and end apart: 2, of which 2 were waited for; matrix products, arithmetic and copies ran while one was open for 1% of the time, Pallas kernels for 0%

commit v1 on v0

--- a/solution.py
+++ b/solution.py
@@ -33,7 +33,15 @@
         axis=0,
     )
     stacked = jnp.transpose(panels, (1, 0, 2)).reshape(share_rows, members * local_cols)
-    gathered = lax.all_gather(stacked, "row", axis=0, tiled=True)
+    gathered = jnp.concatenate(
+        jax.lax.all_to_all(
+            jnp.stack([stacked] * jax.lax.axis_size("row")),
+            axis_name="row",
+            split_axis=0,
+            concat_axis=0,
+        ),
+        0,
+    )
     gathered = gathered.reshape(panel_width, members, local_cols)
     partial_value = jnp.einsum(
         "kmj,ij->mki", gathered, anc_inv, precision=highest, preferred_element_type=jnp.float32

time: 277 us -> 326 us (1.18)
  waiting for transfers between devices: 225 us -> 263 us
  starting transfers between devices: 0.08 us -> 16.7 us
  matrix products: 17.2 us -> 12.1 us
    all_to_all x0 -> x1, waiting for transfers between devices: none -> 173 us  [local(): jax.lax.all_to_all(jnp.stack([stacked] * jax.lax.axis_size('row')), axis_...]
    all_gather x1 -> x0, waiting for transfers between devices: 139 us -> none  [local(): gathered = lax.all_gather(stacked, 'row', axis=0, tiled=True)]
    all_to_all x0 -> x1, starting transfers between devices: none -> 16.7 us  [local(): jax.lax.all_to_all(jnp.stack([stacked] * jax.lax.axis_size('row')), axis_...]
    another operation x0 -> x2, local copies, waits for them, and re-layouts: none -> 8.23 us  [the longest x1 6.1 us: local(): gathered = gathered.reshape(panel_width, members, local_cols)]
    all_gather x1 -> x0, local copies, waits for them, and re-layouts: 5.45 us -> none  [local(): gathered = lax.all_gather(stacked, 'row', axis=0, tiled=True)]
    dot_general x1, matrix products: 14.7 us -> 9.62 us  [local(): jnp.einsum('kmj,ij->mki', gathered, anc_inv, precision=highest, preferred...]
    reduce_scatter x1, waiting for transfers between devices: 85.7 us -> 90.2 us  [local(): reduced = lax.psum_scatter(combined, 'col', scatter_dimension=1, tiled=True)]
  transfers between devices with their start and end apart: 2 -> 2, of which waited for: 2 -> 2; matrix products, arithmetic and copies ran while one was open for 1% -> 0% of each run, Pallas kernels for 0% -> 0%
where the time goes in v1:
time: 326 us
  waiting for transfers between devices  263 us (81%)
  starting transfers between devices  16.7 us (5%)
  between operations  14.2 us (4%)
  matrix products  12.1 us (4%)
  local copies, waits for them, and re-layouts  11.4 us (3%)
  other arithmetic  8.11 us (2%)
    all_to_all x1, waiting for transfers between devices, local(): jax.lax.all_to_all(jnp.stack([stacked] * jax.lax.axis_size('row')), axis_...  173 us
    reduce_scatter x1, waiting for transfers between devices, local(): reduced = lax.psum_scatter(combined, 'col', scatter_dimension=1, tiled=True)  90.2 us
    all_to_all x1, starting transfers between devices, local(): jax.lax.all_to_all(jnp.stack([stacked] * jax.lax.axis_size('row')), axis_...  16.7 us
    dot_general x1, matrix products, local(): jnp.einsum('kmj,ij->mki', gathered, anc_inv, precision=highest, preferred...  9.62 us
  transfers between devices with their start and end apart: 2, of which 2 were waited for; matrix products, arithmetic and copies ran while one was open for 0% of the time, Pallas kernels for 0%

profile of v1, /device:TPU:8, one launch (start us, length us, event | category | flops | bytes accessed | tf_op | source)
XLA Modules:
  0.0 325.5 jit_solution(8689190173792072859)
XLA Ops:
  7.2 0.0 copy-start
  7.2 0.9 compare_reduce_fusion
  8.1 0.8 compare_reduce_fusion.1
  8.9 0.9 broadcast_multiply_fusion
  9.8 0.8 broadcast_multiply_fusion.1
  10.6 2.1 stack.3
  12.8 0.0 copy-start.2
  12.8 0.0 copy-start.4
  12.8 16.7 %all-to-all-start = ((f32[32,8,3840]{2,1,0:T(8,128)}), f32[32,8,3840]{2,1,0:T(8,128)}, u32[]{:S(2)}, u32[]{:S(2)}) async-start(f32[32,8,3840]{2,1,0:T(8,128)} %stack.3), calls=%async_computation | async-start | bytes 7864320 | tf_op jit(solution)/shard_map/all_to_all | solution.py:37
  29.4 0.0 reduce-scatter.2.cloned.1.call-start
  29.5 0.0 copy-done.2
  29.5 0.1 compare_reduce_fusion.2
  29.6 0.0 copy-done.4
  29.7 0.6 gather_fusion
  30.3 0.1 broadcast_select_fusion
  30.3 172.7 %all-to-all-done = f32[32,8,3840]{2,1,0:T(8,128)} async-done(((f32[32,8,3840]{2,1,0:T(8,128)}), f32[32,8,3840]{2,1,0:T(8,128)}, u32[]{:S(2)}, u32[]{:S(2)}) %all-to-all-start) | async-done | bytes 3932192 | tf_op jit(solution)/shard_map/all_to_all | solution.py:37
  203.1 6.1 %reshape_reshape.3 = f32[256,5,768]{2,1,0:T(8,128)} reshape(f32[32,8,3840]{2,1,0:T(8,128)} %all-to-all-done) | data formatting | bytes 7864320 | tf_op jit(solution)/shard_map/reshape;reshape | solution.py:45
  209.2 0.0 copy-done
  209.2 9.6 %fusion.2 = f32[5,256,384]{2,1,0:T(8,128)S(1)} fusion(f32[256,5,768]{2,1,0:T(8,128)} %reshape_reshape.3, f32[384,768]{1,0:T(8,128)S(1)} %copy-done), kind=kOutput, calls=%fused_computation.5 | convolution fusion | flops 4529848320 | bytes 7077888 | tf_op jit(solution)/shard_map/kmj,ij->mki/dot_general | solution.py:46
  218.8 0.0 copy-start.1
  218.8 1.3 copy-done.1
  220.1 0.1 slice.20
  220.1 0.6 gather_fusion.1
  220.8 2.5 fusion.6
  223.3 1.4 pad_maximum_fusion
  224.7 0.0 copy-start.3
  224.7 0.0 reduce-scatter.2.cloned.1.call-update
  224.7 0.7 copy-done.3
  225.4 0.1 compare_reduce_fusion.3
  225.5 90.2 %reduce-scatter.2.cloned.1.call-done = f32[5,16,384]{2,1,0:T(8,128)} async-done(((f32[5,256,384]{2,1,0:T(8,128)}), f32[5,16,384]{2,1,0:T(8,128)}) %reduce-scatter.2.cloned.1.call-update) | async-done | bytes 122896 | tf_op jit(solution)/shard_map/reduce_scatter | solution.py:56
  315.7 1.5 slice_multiply_fusion
  317.2 1.4 slice_multiply_fusion.1
  (11 shorter events, 0.1 us)
Async XLA Ops:
  7.2 202.0 %copy-start = (f32[384,768]{1,0:T(8,128)S(1)}, f32[384,768]{1,0:T(8,128)}, u32[]{:S(2)}) copy-start(f32[384,768]{1,0:T(8,128)} %param.7) | copy-start | bytes 3538948
  12.8 16.7 %copy-start.2 = (s32[3,36]{1,0:T(4,128)S(1)}, s32[3,36]{1,0:T(4,128)}, u32[]{:S(2)}) copy-start(s32[3,36]{1,0:T(4,128)} %param.10) | copy-start | bytes 1300
  12.8 16.9 %copy-start.4 = (s32[2]{0:T(128)S(1)}, s32[2]{0:T(128)}, u32[]{:S(2)}) copy-start(s32[2]{0:T(128)} %param.12) | copy-start | bytes 28
  12.8 190.3 %all-to-all-start = ((f32[32,8,3840]{2,1,0:T(8,128)}), f32[32,8,3840]{2,1,0:T(8,128)}, u32[]{:S(2)}, u32[]{:S(2)}) async-start(f32[32,8,3840]{2,1,0:T(8,128)} %stack.3), calls=%async_computation | async-start | bytes 7864320 | tf_op jit(solution)/shard_map/all_to_all | solution.py:37
  29.4 286.3 %reduce-scatter.2.cloned.1.call-start = ((), (), s32[]{:S(2)}) async-start(), calls=%async_computation.2 | async-start | bytes 2088960 | tf_op jit(solution)/shard_map/reduce_scatter | solution.py:56
  218.8 1.3 copy-start.1
  224.7 0.7 copy-start.3
Sparse Core Ops, SparseCore 0:
  224.8 90.8 reduce-scatter.1
